TPU v7x, 32 devices: a whole 2x2x4 slice. The times are simulated.
32 devices in a mesh: slab: 2 (over x), run: 2 (over core), tx: 8 (over z, y).
Axes of the slice: x: 2, y: 2, z: 4, core: 2. Of those that a mesh axis runs over, the one named last changes fastest.
Arguments:
- snapshots: bfloat16 [1024, 128, 512], P(('slab', 'tx'), None, 'run'), parts along dimension 0, may hold values from -60 to 60, as said below
- coefficient: float32 [1024, 128], P(('slab', 'tx')), parts along dimension 0, may hold values from 0.02 to 0.2
- start_first: int32 [512, 128], replicated, may hold values from -4 to 4
- start_merge: int32 [256, 128], replicated, may hold values from -4 to 4
Outputs:
- modes: float32 [1024, 128, 128], P(('slab', 'tx'), None, 'run'), parts along dimension 0
There are 2 independent parts, one for each index of `slab`. A program takes and returns all parts, laid end to end along the dimension named above; an argument that names none is the same for every part. Nothing has to cross between parts.
Inputs may be any that keep to these rules, and one draw needn't show every extreme that they name: `snapshots`: snapshot values are real-valued and bounded.
All inputs are finite; a program needn't handle non-finite values.
Results may differ from a plain program's by a relative error of at most 0.0003.
Values may be sent and summed in bfloat16 or wider, within the bound.
No kernel may reach another device: no remote copies, remote signals or barrier semaphores. Data moves between devices by JAX's collectives and lax.ppermute only.
A program may use at most 128 MiB of HBM per device.

v0:
```python
import jax
import jax.numpy as jnp
from jax import lax
from jax.sharding import PartitionSpec as P

ITERS = 2
highest = lax.Precision.HIGHEST


def padded_2(block, sides, width):
    for axis, dim in sides:
        count = lax.axis_size(axis)
        forward = [(i, i + 1) for i in range(count - 1)]
        backward = [(target, source) for source, target in forward]
        low = lax.ppermute(
            lax.slice_in_dim(block, block.shape[dim] - width, None, axis=dim), axis, forward
        )
        high = lax.ppermute(lax.slice_in_dim(block, 0, width, axis=dim), axis, backward)
        block = jnp.concatenate([low, block, high], axis=dim)
    return block


def partner(block, axis, stride):
    count = lax.axis_size(axis)
    route = []
    for low in range(count):
        high = low | 1 << stride
        if high != low and high < count:
            route += [(low, high), (high, low)]
    return lax.ppermute(block, axis, route)


def fourth_order(values, axis_dim):
    length_kept = values.shape[axis_dim] - 4

    def shifted(offset):
        return lax.slice_in_dim(values, offset, offset + length_kept, axis=axis_dim)

    return (8.0 * (shifted(3) - shifted(1)) - (shifted(4) - shifted(0))) / 12.0


def fluxes(extended, coefficient):
    squared = 0.5 * jnp.square(extended.astype(jnp.float32))
    along_rows = fourth_order(squared, 0)
    padded = jnp.pad(squared[2:-2], ((0, 0), (2, 2), (0, 0)))
    along_cols = fourth_order(padded, 1)
    central = extended[2:-2].astype(jnp.float32)
    return central - coefficient[:, :, None] * (along_rows + along_cols)


def orthonormal(matrix):
    inner_gram = jnp.dot(matrix.T, matrix, precision=highest)
    factor = jnp.linalg.cholesky(inner_gram)
    return jax.scipy.linalg.solve_triangular(factor, matrix.T, lower=True).T


def iterate(gram_matrix, start_int):
    basis_set = orthonormal(start_int.astype(jnp.float32))
    for sweep_index in range(ITERS):
        basis_set = orthonormal(jnp.dot(gram_matrix, basis_set, precision=highest))
    return basis_set


def cross_gram(left_rows, right_rows):
    return lax.dot_general(left_rows, right_rows, (((0,), (0,)), ((), ())), precision=highest)


def on_device(snapshots, coefficient, start_first, start_merge):
    extended = padded_2(snapshots, (("tx", 0),), 2)
    rows_here = snapshots.shape[0] * snapshots.shape[1]
    order_size = snapshots.shape[2]
    modes_count = start_first.shape[1]
    share_count = modes_count // lax.axis_size("run")
    cells_total = rows_here * lax.axis_size("tx")
    member = lax.axis_index("run")
    is_first = member == 0
    own_start = lax.dynamic_slice_in_dim(start_first, member * order_size, order_size, 0)
    own_flux = fluxes(extended, coefficient).reshape(rows_here, order_size)
    own_gram = lax.psum(cross_gram(own_flux, own_flux), "tx") / cells_total
    own_basis = iterate(own_gram, own_start)
    own_modes = jnp.dot(own_flux, own_basis, precision=highest)
    other_modes = partner(own_modes, "run", 0)
    own_block, mixed_block, other_block = lax.psum(
        (
            cross_gram(own_modes, own_modes),
            cross_gram(own_modes, other_modes),
            cross_gram(other_modes, other_modes),
        ),
        "tx",
    )
    own_block = own_block / cells_total
    mixed_block = mixed_block / cells_total
    other_block = other_block / cells_total
    first_block = jnp.where(is_first, own_block, other_block)
    last_block = jnp.where(is_first, other_block, own_block)
    upper_block = jnp.where(is_first, mixed_block, mixed_block.T)
    merge_gram = jnp.concatenate(
        [
            jnp.concatenate([first_block, upper_block], axis=1),
            jnp.concatenate([upper_block.T, last_block], axis=1),
        ],
        axis=0,
    )
    rotation = iterate(merge_gram, start_merge)
    rotation_share = lax.dynamic_slice_in_dim(rotation, member * share_count, share_count, 1)
    top_rows = rotation_share[:modes_count]
    bottom_rows = rotation_share[modes_count:]
    own_rotation = jnp.where(is_first, top_rows, bottom_rows)
    other_rotation = jnp.where(is_first, bottom_rows, top_rows)
    result = jnp.dot(own_modes, own_rotation, precision=highest) + jnp.dot(
        other_modes, other_rotation, precision=highest
    )
    return result.reshape(snapshots.shape[0], snapshots.shape[1], share_count)


def solution(mesh):
    in_specs = (P(("slab", "tx"), None, "run"), P(("slab", "tx"), None), P(), P())
    out_specs = P(("slab", "tx"), None, "run")
    return jax.shard_map(
        on_device, mesh=mesh, in_specs=in_specs, out_specs=out_specs, check_vma=False
    )
```

profile of v0, /device:TPU:0, one launch (start us, length us, event | category | flops | bytes accessed | tf_op | source)
XLA Modules:
  0.0 407.1 jit_solution(16256215032305025658)
XLA Ops:
  8.8 5.5 %collective-permute-start = (bf16[2,128,256]{2,1,0:T(8,128)(2,1)S(1)}, bf16[2,128,256]{2,1,0:T(8,128)(2,1)S(1)}, u32[]{:S(2)}, u32[]{:S(2)}) collective-permute-start(bf16[2,128,256]{2,1,0:T(8,128)(2,1)S(1)} %get-tuple-element.10), channel_id=1, source_target_pairs={{0,1},{1,2},{2,3},{3,4},{4,5},{5,6},{6,7},{8,9},{9,10},{10,11},{11... | collective-permute-start | bytes 393224 | tf_op jit(solution)/shard_map/ppermute | solution.py:15
  16.6 11.7 %cholesky.104 = f32[128,128]{1,0:T(8,128)S(1)} custom-call(f32[128,128]{1,0:T(8,128)S(1)} %fusion.51), custom_call_target="Cholesky" | custom-call | tf_op jit(solution)/shard_map/jit(cholesky)/cholesky | solution.py:53
  32.4 4.1 %slice.64 = f32[64,128,256]{2,1,0:T(8,128)} slice(f32[68,128,256]{2,1,0:T(8,128)S(1)} %multiply_multiply_fusion), slice={[2:66], [0:128], [0:256]} | slice | bytes 16777216 | tf_op jit(solution)/shard_map/slice | solution.py:45
  36.6 18.5 %fusion.3 = f32[64,128,256]{2,1,0:T(8,128)} fusion(f32[68,128,256]{2,1,0:T(8,128)S(1)} %multiply_multiply_fusion, f32[64,128,256]{2,1,0:T(8,128)} %slice.64, bf16[64,128,256]{2,1,0:T(8,128)(2,1)S(1)} %copy-done, f32[64,128]{1,0:T(8,128)S(1)} %broadcast_multiply_fusion.3), kind=kLoop, calls=%fused_computation.6 | loop fusion | flops 25165824 | bytes 54558720 | tf_op jit(solution)/shard_map/sub | solution.py:48
  55.1 17.7 %convolution_bitcast_fusion = f32[256,256]{1,0:T(8,128)} fusion(f32[64,128,256]{2,1,0:T(8,128)} %fusion.3), kind=kOutput, calls=%fused_computation.12 | convolution fusion | flops 6442450944 | bytes 8650752 | tf_op jit(solution)/shard_map/dot_general | solution.py:65
  73.7 9.8 %custom-call.10 = f32[1,128,128]{1,2,0:T(8,128)S(1)} custom-call(f32[1,128,128]{2,1,0:T(8,128)S(1)} %fusion.34), custom_call_target="InvertDiagBlocksLowerTriangular" | custom-call | tf_op jit(solution)/shard_map/jit(_solve_triangular)/triangular_solve | solution.py:54
  83.8 61.4 %all-reduce.5.cloned.1.call-done = f32[256,256]{1,0:T(8,128)} async-done(((f32[256,256]{1,0:T(8,128)}), f32[256,256]{1,0:T(8,128)}) %all-reduce.5.cloned.1.call-update) | async-done | bytes 262160 | tf_op jit(solution)/shard_map/psum | solution.py:79
  147.1 11.7 %cholesky.115 = f32[128,128]{1,0:T(8,128)S(1)} custom-call(f32[128,128]{1,0:T(8,128)S(1)} %fusion.49), custom_call_target="Cholesky" | custom-call | tf_op jit(solution)/shard_map/jit(cholesky)/cholesky | solution.py:53
  160.2 9.8 %custom-call.11 = f32[1,128,128]{1,2,0:T(8,128)S(1)} custom-call(f32[1,128,128]{2,1,0:T(8,128)S(1)} %fusion.35), custom_call_target="InvertDiagBlocksLowerTriangular" | custom-call | tf_op jit(solution)/shard_map/jit(_solve_triangular)/triangular_solve | solution.py:54
  172.2 11.9 %cholesky.126 = f32[128,128]{1,0:T(8,128)S(1)} custom-call(f32[128,128]{1,0:T(8,128)S(1)} %fusion.47), custom_call_target="Cholesky" | custom-call | tf_op jit(solution)/shard_map/jit(cholesky)/cholesky | solution.py:53
  185.4 9.8 %custom-call.12 = f32[1,128,128]{1,2,0:T(8,128)S(1)} custom-call(f32[1,128,128]{2,1,0:T(8,128)S(1)} %fusion.36), custom_call_target="InvertDiagBlocksLowerTriangular" | custom-call | tf_op jit(solution)/shard_map/jit(_solve_triangular)/triangular_solve | solution.py:54
  195.5 10.8 %fusion.74 = f32[8192,128]{1,0:T(8,128)} fusion(f32[8192,256]{1,0:T(8,128)} %bitcast.109, f32[128,256]{1,0:T(8,128)S(1)} %fusion.18), kind=kOutput, calls=%fused_computation.114 | convolution fusion | flops 3221225472 | bytes 12713984 | tf_op jit(solution)/shard_map/dot_general | solution.py:81
  206.9 11.7 %cholesky.137 = f32[128,128]{1,0:T(8,128)S(1)} custom-call(f32[128,128]{1,0:T(8,128)S(1)} %fusion.45), custom_call_target="Cholesky" | custom-call | tf_op jit(solution)/shard_map/jit(cholesky)/cholesky | solution.py:53
  220.0 9.8 %custom-call.13 = f32[1,128,128]{1,2,0:T(8,128)S(1)} custom-call(f32[1,128,128]{2,1,0:T(8,128)S(1)} %fusion.37), custom_call_target="InvertDiagBlocksLowerTriangular" | custom-call | tf_op jit(solution)/shard_map/jit(_solve_triangular)/triangular_solve | solution.py:54
  229.8 11.0 %fusion.75 = f32[128,128]{1,0:T(8,128)} fusion(f32[8192,128]{1,0:T(8,128)} %fusion.74), kind=kOutput, calls=%fused_computation.115 | convolution fusion | flops 1610612736 | bytes 4259840 | tf_op jit(solution)/shard_map/dot_general | solution.py:65
  240.8 10.8 %fusion.76 = f32[128,128]{0,1:T(8,128)} fusion(f32[8192,128]{1,0:T(8,128)} %collective-permute-done.2), kind=kOutput, calls=%fused_computation.116 | convolution fusion | flops 1610612736 | bytes 4259840 | tf_op jit(solution)/shard_map/dot_general | solution.py:65
  251.6 11.0 %fusion.77 = f32[128,128]{0,1:T(8,128)} fusion(f32[8192,128]{1,0:T(8,128)} %fusion.74, f32[8192,128]{1,0:T(8,128)} %collective-permute-done.2), kind=kOutput, calls=%fused_computation.117 | convolution fusion | flops 1610612736 | bytes 8454144 | tf_op jit(solution)/shard_map/dot_general | solution.py:65
  263.0 70.1 %all-reduce.7.cloned.1.call-done = (f32[128,128]{0,1:T(8,128)}, f32[128,128]{1,0:T(8,128)}, f32[128,128]{0,1:T(8,128)}) async-done(((f32[128,128]{0,1:T(8,128)}, f32[128,128]{1,0:T(8,128)}, f32[128,128]{0,1:T(8,128)}), (f32[128,128]{0,1:T(8,128)}, f32[128,128]{1,0:T(8,128)}, f32[128,128]{0,1:T(8,128)})) %all-reduce.7.cloned.1.call-update) | async-done | bytes 196624 | tf_op jit(solution)/shard_map/psum | solution.py:83
  337.9 11.7 %cholesky.148 = f32[128,128]{1,0:T(8,128)S(1)} custom-call(f32[128,128]{1,0:T(8,128)S(1)} %fusion.43), custom_call_target="Cholesky" | custom-call | tf_op jit(solution)/shard_map/jit(cholesky)/cholesky | solution.py:53
  350.9 9.8 %custom-call.14 = f32[1,128,128]{1,2,0:T(8,128)S(1)} custom-call(f32[1,128,128]{2,1,0:T(8,128)S(1)} %fusion.38), custom_call_target="InvertDiagBlocksLowerTriangular" | custom-call | tf_op jit(solution)/shard_map/jit(_solve_triangular)/triangular_solve | solution.py:54
  361.9 11.9 %cholesky.159 = f32[128,128]{1,0:T(8,128)S(1)} custom-call(f32[128,128]{1,0:T(8,128)S(1)} %fusion.41), custom_call_target="Cholesky" | custom-call | tf_op jit(solution)/shard_map/jit(cholesky)/cholesky | solution.py:53
  375.2 9.8 %custom-call.15 = f32[1,128,128]{1,2,0:T(8,128)S(1)} custom-call(f32[1,128,128]{2,1,0:T(8,128)S(1)} %fusion.39), custom_call_target="InvertDiagBlocksLowerTriangular" | custom-call | tf_op jit(solution)/shard_map/jit(_solve_triangular)/triangular_solve | solution.py:54
  385.4 6.4 %fusion.57 = f32[8192,64]{0,1:T(8,128)S(1)} fusion(f32[8192,128]{1,0:T(8,128)} %fusion.74, f32[256,64]{0,1:T(8,128)S(1)} %dynamic-slice_bitcast_fusion, pred[]{:T(512)S(6)} %eq.3), kind=kOutput, calls=%fused_computation.86 | convolution fusion | flops 805314560 | bytes 6356993 | tf_op jit(solution)/shard_map/dot_general | solution.py:110
  391.8 6.4 %fusion.5 = f32[8,64,8,128]{3,2,1,0:T(8,128)S(1)} fusion(f32[8192,64]{0,1:T(8,128)S(1)} %fusion.57, f32[8192,128]{1,0:T(8,128)} %collective-permute-done.2, f32[256,64]{0,1:T(8,128)S(1)} %dynamic-slice_bitcast_fusion, pred[]{:T(512)S(6)} %eq.3), kind=kOutput, calls=%fused_computation.11 | convolution fusion | flops 805838848 | bytes 8454145 | tf_op jit(solution)/shard_map/dot_general | solution.py:110
  (75 shorter events, 29.4 us)
Async XLA Ops:
  6.5 138.7 %all-reduce.5.cloned.1.call-start = ((), (), s32[]{:S(2)}) async-start(), calls=%async_computation | async-start | bytes 524288 | tf_op jit(solution)/shard_map/psum | solution.py:79
  7.5 21.5 %collective-permute-start.1 = (bf16[2,128,256]{2,1,0:T(8,128)(2,1)S(1)}, bf16[2,128,256]{2,1,0:T(8,128)(2,1)S(1)}, u32[]{:S(2)}, u32[]{:S(2)}) collective-permute-start(bf16[2,128,256]{2,1,0:T(8,128)(2,1)S(1)} %get-tuple-element.11), channel_id=1, source_target_pairs={{1,0},{2,1},{3,2},{4,3},{5,4},{6,5},{7,6},{9,8},{10,9},{11,10},{12... | collective-permute-start | bytes 393224 | tf_op jit(solution)/shard_map/ppermute | solution.py:18
  8.8 20.2 %collective-permute-start = (bf16[2,128,256]{2,1,0:T(8,128)(2,1)S(1)}, bf16[2,128,256]{2,1,0:T(8,128)(2,1)S(1)}, u32[]{:S(2)}, u32[]{:S(2)}) collective-permute-start(bf16[2,128,256]{2,1,0:T(8,128)(2,1)S(1)} %get-tuple-element.10), channel_id=1, source_target_pairs={{0,1},{1,2},{2,3},{3,4},{4,5},{5,6},{6,7},{8,9},{9,10},{10,11},{11... | collective-permute-start | bytes 393224 | tf_op jit(solution)/shard_map/ppermute | solution.py:15
  32.4 4.2 %copy-start = (bf16[64,128,256]{2,1,0:T(8,128)(2,1)S(1)}, bf16[64,128,256]{2,1,0:T(8,128)(2,1)}, u32[]{:S(2)}) copy-start(bf16[64,128,256]{2,1,0:T(8,128)(2,1)} %param.7) | copy-start | bytes 12582916
  55.1 28.4 %copy-start.2 = (s32[512,128]{1,0:T(8,128)S(1)}, s32[512,128]{1,0:T(8,128)}, u32[]{:S(2)}) copy-start(s32[512,128]{1,0:T(8,128)} %param.9) | copy-start | bytes 786436
  72.9 260.1 %all-reduce.7.cloned.1.call-start = ((), (), s32[]{:S(2)}) async-start(), calls=%async_computation.1 | async-start | bytes 393216 | tf_op jit(solution)/shard_map/psum | solution.py:83
  195.5 10.9 %copy-start.1 = (s32[256,128]{1,0:T(8,128)S(1)}, s32[256,128]{1,0:T(8,128)}, u32[]{:S(2)}) copy-start(s32[256,128]{1,0:T(8,128)} %param.10) | copy-start | bytes 393220
  206.3 34.5 %collective-permute-start.2 = (f32[8192,128]{1,0:T(8,128)}, f32[8192,128]{1,0:T(8,128)}, u32[]{:S(2)}, u32[]{:S(2)}) collective-permute-start(f32[8192,128]{1,0:T(8,128)} %fusion.74), channel_id=1, source_target_pairs={{0,8},{8,0},{1,9},{9,1},{2,10},{10,2},{3,11},{11,3},{4,12},{12,4},... | collective-permute-start | bytes 12582920 | tf_op jit(solution)/shard_map/ppermute | solution.py:30
Sparse Core Ops, SparseCore 0:
  73.0 72.2 all-reduce.4
  262.8 70.2 all-reduce.6
where the time goes:
time: 411 us; the launch traced here: 407 us
  other arithmetic  164 us (40%)
  waiting for transfers between devices  132 us (32%)
  matrix products  82.7 us (20%)
  between operations  14.3 us (3%)
  local copies, waits for them, and re-layouts  7.74 us (2%)
  starting transfers between devices  7.09 us (2%)
    another operation x18, other arithmetic, orthonormal(): factor = jnp.linalg.cholesky(inner_gram)  74.7 us
    psum x1, waiting for transfers between devices, on_device(): lax.psum((cross_gram(own_modes, own_modes), cross_gram(own_modes, other_m...  70.1 us
    another operation x12, other arithmetic, orthonormal(): return jax.scipy.linalg.solve_triangular(factor, matrix.T, lower=True).T  62.7 us
    psum x1, waiting for transfers between devices, on_device(): own_gram = lax.psum(cross_gram(own_flux, own_flux), 'tx') / cells_total  61.4 us
    dot_general x4, matrix products, cross_gram(): lax.dot_general(left_rows, right_rows, (((0,), (0,)), ((), ())), precisio...  50.6 us
    sub x1, other arithmetic, fluxes(): return central - coefficient[:, :, None] * (along_rows + along_cols)  18.5 us
    dot_general x1, matrix products, on_device(): own_modes = jnp.dot(own_flux, own_basis, precision=highest)  10.8 us
  transfers between devices with their start and end apart: 5, of which 2 were waited for; matrix products, arithmetic and copies ran while one was open for 15% of the time, Pallas kernels for 0%

commit v1 on v0

--- a/solution.py
+++ b/solution.py
@@ -76,7 +76,7 @@
     is_first = member == 0
     own_start = lax.dynamic_slice_in_dim(start_first, member * order_size, order_size, 0)
     own_flux = fluxes(extended, coefficient).reshape(rows_here, order_size)
-    own_gram = lax.psum(cross_gram(own_flux, own_flux), "tx") / cells_total
+    own_gram = jnp.sum(lax.all_gather(cross_gram(own_flux, own_flux), "tx"), axis=0) / cells_total
     own_basis = iterate(own_gram, own_start)
     own_modes = jnp.dot(own_flux, own_basis, precision=highest)
     other_modes = partner(own_modes, "run", 0)

time: 411 us -> 382 us (0.929)
  waiting for transfers between devices: 132 us -> 99.8 us
    psum x1 -> x0, waiting for transfers between devices: 61.4 us -> none  [on_device(): own_gram = lax.psum(cross_gram(own_flux, own_flux), 'tx') / cells_total]
    all_gather x0 -> x1, waiting for transfers between devices: none -> 26.8 us  [on_device(): lax.all_gather(cross_gram(own_flux, own_flux), 'tx')]
  transfers between devices with their start and end apart: 5 -> 5, of which waited for: 2 -> 4; matrix products, arithmetic and copies ran while one was open for 15% -> 16% of each run, Pallas kernels for 0% -> 0%
where the time goes in v1:
time: 382 us; the launch traced here: 374 us
  other arithmetic  165 us (43%)
  waiting for transfers between devices  99.8 us (26%)
  matrix products  79.9 us (21%)
  between operations  14.3 us (4%)
  local copies, waits for them, and re-layouts  7.74 us (2%)
  starting transfers between devices  7.38 us (2%)
    another operation x18, other arithmetic, orthonormal(): factor = jnp.linalg.cholesky(inner_gram)  74.6 us
    psum x1, waiting for transfers between devices, on_device(): lax.psum((cross_gram(own_modes, own_modes), cross_gram(own_modes, other_m...  69.3 us
    another operation x12, other arithmetic, orthonormal(): return jax.scipy.linalg.solve_triangular(factor, matrix.T, lower=True).T  63 us
    dot_general x4, matrix products, cross_gram(): lax.dot_general(left_rows, right_rows, (((0,), (0,)), ((), ())), precisio...  50.6 us
    all_gather x1, waiting for transfers between devices, on_device(): lax.all_gather(cross_gram(own_flux, own_flux), 'tx')  26.8 us
    sub x1, other arithmetic, fluxes(): return central - coefficient[:, :, None] * (along_rows + along_cols)  18.5 us
    dot_general x1, matrix products, on_device(): own_modes = jnp.dot(own_flux, own_basis, precision=highest)  10.8 us
  transfers between devices with their start and end apart: 5, of which 4 were waited for; matrix products, arithmetic and copies ran while one was open for 16% of the time, Pallas kernels for 0%

profile of v1, /device:TPU:0, one launch (start us, length us, event | category | flops | bytes accessed | tf_op | source)
XLA Modules:
  0.0 374.3 jit_solution(873098190737890891)
XLA Ops:
  8.8 5.5 %collective-permute-start = (bf16[2,128,256]{2,1,0:T(8,128)(2,1)S(1)}, bf16[2,128,256]{2,1,0:T(8,128)(2,1)S(1)}, u32[]{:S(2)}, u32[]{:S(2)}) collective-permute-start(bf16[2,128,256]{2,1,0:T(8,128)(2,1)S(1)} %get-tuple-element.10), channel_id=1, source_target_pairs={{0,1},{1,2},{2,3},{3,4},{4,5},{5,6},{6,7},{8,9},{9,10},{10,11},{11... | collective-permute-start | bytes 393224 | tf_op jit(solution)/shard_map/ppermute | solution.py:15
  21.8 4.1 %slice.64 = f32[64,128,256]{2,1,0:T(8,128)} slice(f32[68,128,256]{2,1,0:T(8,128)S(1)} %multiply_multiply_fusion), slice={[2:66], [0:128], [0:256]} | slice | bytes 16777216 | tf_op jit(solution)/shard_map/slice | solution.py:45
  26.0 18.5 %fusion.3 = f32[64,128,256]{2,1,0:T(8,128)} fusion(f32[68,128,256]{2,1,0:T(8,128)S(1)} %multiply_multiply_fusion, f32[64,128,256]{2,1,0:T(8,128)} %slice.64, bf16[64,128,256]{2,1,0:T(8,128)(2,1)S(1)} %copy-done, f32[64,128]{1,0:T(8,128)S(1)} %broadcast_multiply_fusion.3), kind=kLoop, calls=%fused_computation.6 | loop fusion | flops 25165824 | bytes 54558720 | tf_op jit(solution)/shard_map/sub | solution.py:48
  44.5 17.7 %convolution_bitcast_fusion = f32[256,256]{1,0:T(8,128)} fusion(f32[64,128,256]{2,1,0:T(8,128)} %fusion.3), kind=kOutput, calls=%fused_computation.12 | convolution fusion | flops 6442450944 | bytes 8650752 | tf_op jit(solution)/shard_map/dot_general | solution.py:65
  63.4 11.7 %cholesky.104 = f32[128,128]{1,0:T(8,128)S(1)} custom-call(f32[128,128]{1,0:T(8,128)S(1)} %fusion.51), custom_call_target="Cholesky" | custom-call | tf_op jit(solution)/shard_map/jit(cholesky)/cholesky | solution.py:53
  76.5 9.8 %custom-call.10 = f32[1,128,128]{1,2,0:T(8,128)S(1)} custom-call(f32[1,128,128]{2,1,0:T(8,128)S(1)} %fusion.34), custom_call_target="InvertDiagBlocksLowerTriangular" | custom-call | tf_op jit(solution)/shard_map/jit(_solve_triangular)/triangular_solve | solution.py:54
  86.6 26.8 %all-gather.3.cloned.1.call-done = f32[2048,256]{1,0:T(8,128)} async-done(((f32[256,256]{1,0:T(8,128)}), f32[2048,256]{1,0:T(8,128)}) %all-gather.3.cloned.1.call-update) | async-done | bytes 2097168 | tf_op jit(solution)/shard_map/all_gather | solution.py:79
  116.1 11.7 %cholesky.115 = f32[128,128]{1,0:T(8,128)S(1)} custom-call(f32[128,128]{1,0:T(8,128)S(1)} %fusion.49), custom_call_target="Cholesky" | custom-call | tf_op jit(solution)/shard_map/jit(cholesky)/cholesky | solution.py:53
  129.1 10.0 %custom-call.11 = f32[1,128,128]{1,2,0:T(8,128)S(1)} custom-call(f32[1,128,128]{2,1,0:T(8,128)S(1)} %fusion.35), custom_call_target="InvertDiagBlocksLowerTriangular" | custom-call | tf_op jit(solution)/shard_map/jit(_solve_triangular)/triangular_solve | solution.py:54
  140.3 11.7 %cholesky.126 = f32[128,128]{1,0:T(8,128)S(1)} custom-call(f32[128,128]{1,0:T(8,128)S(1)} %fusion.47), custom_call_target="Cholesky" | custom-call | tf_op jit(solution)/shard_map/jit(cholesky)/cholesky | solution.py:53
  153.3 9.8 %custom-call.12 = f32[1,128,128]{1,2,0:T(8,128)S(1)} custom-call(f32[1,128,128]{2,1,0:T(8,128)S(1)} %fusion.36), custom_call_target="InvertDiagBlocksLowerTriangular" | custom-call | tf_op jit(solution)/shard_map/jit(_solve_triangular)/triangular_solve | solution.py:54
  163.5 10.8 %fusion.74 = f32[8192,128]{1,0:T(8,128)} fusion(f32[8192,256]{1,0:T(8,128)} %bitcast.110, f32[128,256]{1,0:T(8,128)S(1)} %fusion.18), kind=kOutput, calls=%fused_computation.114 | convolution fusion | flops 3221225472 | bytes 12713984 | tf_op jit(solution)/shard_map/dot_general | solution.py:81
  174.9 11.7 %cholesky.137 = f32[128,128]{1,0:T(8,128)S(1)} custom-call(f32[128,128]{1,0:T(8,128)S(1)} %fusion.45), custom_call_target="Cholesky" | custom-call | tf_op jit(solution)/shard_map/jit(cholesky)/cholesky | solution.py:53
  187.9 9.8 %custom-call.13 = f32[1,128,128]{1,2,0:T(8,128)S(1)} custom-call(f32[1,128,128]{2,1,0:T(8,128)S(1)} %fusion.37), custom_call_target="InvertDiagBlocksLowerTriangular" | custom-call | tf_op jit(solution)/shard_map/jit(_solve_triangular)/triangular_solve | solution.py:54
  197.7 11.0 %fusion.75 = f32[128,128]{1,0:T(8,128)} fusion(f32[8192,128]{1,0:T(8,128)} %fusion.74), kind=kOutput, calls=%fused_computation.115 | convolution fusion | flops 1610612736 | bytes 4259840 | tf_op jit(solution)/shard_map/dot_general | solution.py:65
  208.7 10.8 %fusion.76 = f32[128,128]{0,1:T(8,128)} fusion(f32[8192,128]{1,0:T(8,128)} %collective-permute-done.2), kind=kOutput, calls=%fused_computation.116 | convolution fusion | flops 1610612736 | bytes 4259840 | tf_op jit(solution)/shard_map/dot_general | solution.py:65
  219.5 11.0 %fusion.77 = f32[128,128]{0,1:T(8,128)} fusion(f32[8192,128]{1,0:T(8,128)} %fusion.74, f32[8192,128]{1,0:T(8,128)} %collective-permute-done.2), kind=kOutput, calls=%fused_computation.117 | convolution fusion | flops 1610612736 | bytes 8454144 | tf_op jit(solution)/shard_map/dot_general | solution.py:65
  230.9 69.3 %all-reduce.4.cloned.1.call-done = (f32[128,128]{0,1:T(8,128)}, f32[128,128]{1,0:T(8,128)}, f32[128,128]{0,1:T(8,128)}) async-done(((f32[128,128]{0,1:T(8,128)}, f32[128,128]{1,0:T(8,128)}, f32[128,128]{0,1:T(8,128)}), (f32[128,128]{0,1:T(8,128)}, f32[128,128]{1,0:T(8,128)}, f32[128,128]{0,1:T(8,128)})) %all-reduce.4.cloned.1.call-update) | async-done | bytes 196624 | tf_op jit(solution)/shard_map/psum | solution.py:83
  305.0 11.7 %cholesky.148 = f32[128,128]{1,0:T(8,128)S(1)} custom-call(f32[128,128]{1,0:T(8,128)S(1)} %fusion.43), custom_call_target="Cholesky" | custom-call | tf_op jit(solution)/shard_map/jit(cholesky)/cholesky | solution.py:53
  318.1 9.8 %custom-call.14 = f32[1,128,128]{1,2,0:T(8,128)S(1)} custom-call(f32[1,128,128]{2,1,0:T(8,128)S(1)} %fusion.38), custom_call_target="InvertDiagBlocksLowerTriangular" | custom-call | tf_op jit(solution)/shard_map/jit(_solve_triangular)/triangular_solve | solution.py:54
  329.1 11.9 %cholesky.159 = f32[128,128]{1,0:T(8,128)S(1)} custom-call(f32[128,128]{1,0:T(8,128)S(1)} %fusion.41), custom_call_target="Cholesky" | custom-call | tf_op jit(solution)/shard_map/jit(cholesky)/cholesky | solution.py:53
  342.4 9.8 %custom-call.15 = f32[1,128,128]{1,2,0:T(8,128)S(1)} custom-call(f32[1,128,128]{2,1,0:T(8,128)S(1)} %fusion.39), custom_call_target="InvertDiagBlocksLowerTriangular" | custom-call | tf_op jit(solution)/shard_map/jit(_solve_triangular)/triangular_solve | solution.py:54
  352.5 6.4 %fusion.57 = f32[8192,64]{0,1:T(8,128)S(1)} fusion(f32[8192,128]{1,0:T(8,128)} %fusion.74, f32[256,64]{0,1:T(8,128)S(1)} %dynamic-slice_bitcast_fusion, pred[]{:T(512)S(6)} %eq.3), kind=kOutput, calls=%fused_computation.86 | convolution fusion | flops 805314560 | bytes 6356993 | tf_op jit(solution)/shard_map/dot_general | solution.py:110
  359.0 6.4 %fusion.5 = f32[8,64,8,128]{3,2,1,0:T(8,128)S(1)} fusion(f32[8192,64]{0,1:T(8,128)S(1)} %fusion.57, f32[8192,128]{1,0:T(8,128)} %collective-permute-done.2, f32[256,64]{0,1:T(8,128)S(1)} %dynamic-slice_bitcast_fusion, pred[]{:T(512)S(6)} %eq.3), kind=kOutput, calls=%fused_computation.11 | convolution fusion | flops 805838848 | bytes 8454145 | tf_op jit(solution)/shard_map/dot_general | solution.py:110
  (76 shorter events, 32.1 us)
Async XLA Ops:
  6.5 106.9 %all-gather.3.cloned.1.call-start = ((), (), s32[]{:S(2)}) async-start(), calls=%async_computation | async-start | bytes 2359296 | tf_op jit(solution)/shard_map/all_gather | solution.py:79
  7.5 8.4 %collective-permute-start.1 = (bf16[2,128,256]{2,1,0:T(8,128)(2,1)S(1)}, bf16[2,128,256]{2,1,0:T(8,128)(2,1)S(1)}, u32[]{:S(2)}, u32[]{:S(2)}) collective-permute-start(bf16[2,128,256]{2,1,0:T(8,128)(2,1)S(1)} %get-tuple-element.11), channel_id=1, source_target_pairs={{1,0},{2,1},{3,2},{4,3},{5,4},{6,5},{7,6},{9,8},{10,9},{11,10},{12... | collective-permute-start | bytes 393224 | tf_op jit(solution)/shard_map/ppermute | solution.py:18
  8.8 10.0 %collective-permute-start = (bf16[2,128,256]{2,1,0:T(8,128)(2,1)S(1)}, bf16[2,128,256]{2,1,0:T(8,128)(2,1)S(1)}, u32[]{:S(2)}, u32[]{:S(2)}) collective-permute-start(bf16[2,128,256]{2,1,0:T(8,128)(2,1)S(1)} %get-tuple-element.10), channel_id=1, source_target_pairs={{0,1},{1,2},{2,3},{3,4},{4,5},{5,6},{6,7},{8,9},{9,10},{10,11},{11... | collective-permute-start | bytes 393224 | tf_op jit(solution)/shard_map/ppermute | solution.py:15
  21.8 4.2 %copy-start = (bf16[64,128,256]{2,1,0:T(8,128)(2,1)S(1)}, bf16[64,128,256]{2,1,0:T(8,128)(2,1)}, u32[]{:S(2)}) copy-start(bf16[64,128,256]{2,1,0:T(8,128)(2,1)} %param.7) | copy-start | bytes 12582916
  44.5 18.3 %copy-start.2 = (s32[512,128]{1,0:T(8,128)S(1)}, s32[512,128]{1,0:T(8,128)}, u32[]{:S(2)}) copy-start(s32[512,128]{1,0:T(8,128)} %param.9) | copy-start | bytes 786436
  62.3 237.9 %all-reduce.4.cloned.1.call-start = ((), (), s32[]{:S(2)}) async-start(), calls=%async_computation.1 | async-start | bytes 393216 | tf_op jit(solution)/shard_map/psum | solution.py:83
  163.5 10.9 %copy-start.1 = (s32[256,128]{1,0:T(8,128)S(1)}, s32[256,128]{1,0:T(8,128)}, u32[]{:S(2)}) copy-start(s32[256,128]{1,0:T(8,128)} %param.10) | copy-start | bytes 393220
  174.3 34.5 %collective-permute-start.2 = (f32[8192,128]{1,0:T(8,128)}, f32[8192,128]{1,0:T(8,128)}, u32[]{:S(2)}, u32[]{:S(2)}) collective-permute-start(f32[8192,128]{1,0:T(8,128)} %fusion.74), channel_id=1, source_target_pairs={{0,8},{8,0},{1,9},{9,1},{2,10},{10,2},{3,11},{11,3},{4,12},{12,4},... | collective-permute-start | bytes 12582920 | tf_op jit(solution)/shard_map/ppermute | solution.py:30
Sparse Core Ops, SparseCore 0:
  62.4 50.9 all-gather.2
  230.7 69.4 all-reduce.3
